TPU v7x, 128 devices: a whole 4x4x4 slice. The times are simulated.
128 devices in a mesh: seq: 32 (over x, y, core), fsdp: 4 (over z).
Axes of the slice: x: 4, y: 4, z: 4, core: 2. Of those that a mesh axis runs over, the one named last changes fastest.
Arguments:
- patches: bfloat16 [32768, 1280], P(('seq', 'fsdp')), may hold values from -6 to 6
- vis_index: int32 [32768], P(('seq', 'fsdp')), may hold values from 0 to 131071, as said below
- kv_list: int32 [256, 16], P(('seq', 'fsdp')), may hold values from 0 to 255, as said below
- kv_count: int32 [256], P(('seq', 'fsdp')), may hold values from 1 to 16, as said below
- global_tiles: int32 [2], replicated, may hold values from 0 to 255
- frame_table: bfloat16 [256, 1280], replicated, may hold values from -3 to 3
- space_table: bfloat16 [512, 1280], replicated, may hold values from -3 to 3
- ln_gain: bfloat16 [1280], replicated, may hold values from 0.25 to 1.75
- ln_bias: bfloat16 [1280], replicated, may hold values from -3 to 3
- w_qkv: bfloat16 [1280, 3840], P('fsdp')
- w_out: bfloat16 [1280, 1280], P('fsdp'), may hold values from -1.25 to 1.25
Outputs:
- attended: bfloat16 [32768, 1280], P(('seq', 'fsdp'))
Inputs may be any that keep to these rules, and one draw needn't show every extreme that they name: `vis_index`: exactly one visible position in each aligned group of four; strictly increasing. `kv_list`: the first entry of query tile i is i itself; entries may repeat; every entry t satisfies |t // 8 - i // 8| <= 2. Over all entries of an aligned run of 2 query tiles, the tiles that lie in any one group other than the run's own group (group = tile // 8) number at most 3 distinct ones, and exactly 3 for every such group within two of the run's own. On every device at least one query tile has kv_count = 16.
All inputs are finite; a program needn't handle non-finite values.
Results may differ from a plain program's by a relative error of at most 0.0065.
Values may be sent and summed in bfloat16 or wider, within the bound.
No kernel may reach another device: no remote copies, remote signals or barrier semaphores. Data moves between devices by JAX's collectives and lax.ppermute only.
A program may use at most 192 MiB of HBM per device.

v0:
```python
import jax
import jax.numpy as jnp
from jax import lax
from jax.sharding import PartitionSpec as P

HEADS = 16
TILE = 128
KT = 16
GLOBAL = 2
PATCHES = 512
NEAR = 3
REACH = (-2, -1, 1, 2)


def passed_along(block, axis, distance):
    devices = range(lax.axis_size(axis))
    route = [(i - distance, i) for i in devices if i - distance in devices]
    return lax.ppermute(block, axis, route)


def layer_norm(stream, ln_gain, ln_bias):
    stream32 = stream.astype(jnp.float32)
    mean_val = jnp.mean(stream32, axis=-1, keepdims=True)
    centred = stream32 - mean_val
    variance = jnp.mean(centred * centred, axis=-1, keepdims=True)
    scaled = centred * lax.rsqrt(variance + 1e-06)
    return (scaled * ln_gain.astype(jnp.float32) + ln_bias.astype(jnp.float32)).astype(jnp.bfloat16)


def embed(patches, vis_index, frame_table, space_table):
    frame_ids = vis_index // PATCHES
    patch_ids = vis_index % PATCHES
    return (
        patches.astype(jnp.float32)
        + frame_table[frame_ids].astype(jnp.float32)
        + space_table[patch_ids].astype(jnp.float32)
    ).astype(jnp.bfloat16)


def near_tiles(entries, group, group_tiles):
    cand = group * group_tiles + jnp.arange(group_tiles, dtype=jnp.int32)
    named = jnp.any(entries.reshape(-1, 1) == cand[None, :], axis=0)
    rank = jnp.cumsum(named.astype(jnp.int32)) - 1
    local_ids = jnp.arange(group_tiles, dtype=jnp.int32)
    picks = jnp.stack([jnp.sum(jnp.where(named & (rank == j), local_ids, 0)) for j in range(NEAR)])
    return (picks, rank)


def attend_tile(query_tile, key_values, key_live, feat_width):
    head_size = feat_width // HEADS
    key_rows = key_values.shape[0]
    queries_h = query_tile.reshape(TILE, HEADS, head_size)
    keys_h = key_values[:, :feat_width].reshape(key_rows, HEADS, head_size)
    values_h = key_values[:, feat_width:].reshape(key_rows, HEADS, head_size)
    scores = jnp.einsum(
        "qhd,khd->hqk", queries_h, keys_h, preferred_element_type=jnp.float32
    ) * head_size ** (-0.5)
    scores = jnp.where(key_live[None, None, :], scores, -jnp.inf)
    row_max = jnp.max(scores, axis=-1, keepdims=True)
    weights_raw = jnp.exp(scores - row_max)
    probs = (weights_raw / jnp.sum(weights_raw, axis=-1, keepdims=True)).astype(jnp.bfloat16)
    mixed_h = jnp.einsum("hqk,khd->qhd", probs, values_h, preferred_element_type=jnp.float32)
    return mixed_h.reshape(TILE, feat_width).astype(jnp.bfloat16)


def local(
    patches,
    vis_index,
    kv_list,
    kv_count,
    global_tiles,
    frame_table,
    space_table,
    ln_gain,
    ln_bias,
    w_qkv,
    w_out,
):
    tok_rows = patches.shape[0]
    feat_width = patches.shape[1]
    tile_count = tok_rows // TILE
    fsdp_size = lax.axis_size("fsdp")
    seq_size = lax.axis_size("seq")
    seq_at = lax.axis_index("seq")
    dev_at = seq_at * fsdp_size + lax.axis_index("fsdp")
    group_tiles = tile_count * fsdp_size
    stream = embed(patches, vis_index, frame_table, space_table)
    dev_count = seq_size * fsdp_size
    global_rows = []
    owners = []
    for slot_no in range(GLOBAL):
        tile_id = global_tiles[slot_no]
        owners.append(tile_id // tile_count)
        global_rows.append(lax.dynamic_slice_in_dim(stream, tile_id % tile_count * TILE, TILE, 0))
    global_stream = jnp.stack(global_rows)
    owners = jnp.stack(owners)
    bit_order = sorted(range(dev_count.bit_length() - 1), key=lambda b: -b)
    done_bits = 0
    for bit in bit_order:
        step = 1 << bit
        held = (dev_at ^ owners) & ~done_bits == 0
        got = lax.ppermute(
            global_stream, ("seq", "fsdp"), [(i, i ^ step) for i in range(dev_count)]
        )
        global_stream = jnp.where(held[:, None, None], global_stream, got)
        done_bits |= step
    global_stream = global_stream.reshape(GLOBAL * TILE, feat_width)
    w_full = lax.all_gather(w_qkv, "fsdp", axis=0, tiled=True)
    normed = layer_norm(stream, ln_gain, ln_bias)
    qkv = jnp.dot(normed, w_full, preferred_element_type=jnp.float32).astype(jnp.bfloat16)
    query = qkv[:, :feat_width]
    keyval = qkv[:, feat_width:]
    global_normed = layer_norm(global_stream, ln_gain, ln_bias)
    global_kv = (
        jnp.dot(global_normed, w_full[:, feat_width:], preferred_element_type=jnp.float32)
        .astype(jnp.bfloat16)
        .reshape(GLOBAL, TILE, 2 * feat_width)
    )
    group_block = lax.all_gather(keyval, "fsdp", axis=0, tiled=True).reshape(
        group_tiles, TILE, 2 * feat_width
    )
    near_blocks = []
    near_rank = []
    for reach in REACH:
        picks, rank = near_tiles(kv_list, seq_at + reach, group_tiles)
        asked = passed_along(picks, "seq", reach)
        near_blocks.append(passed_along(group_block[asked], "seq", -reach))
        near_rank.append(rank)
    window = jnp.concatenate([group_block] + near_blocks + [global_kv], axis=0)
    near_rank = jnp.stack(near_rank)
    entry_group = kv_list // group_tiles
    entry_local = kv_list % group_tiles
    reach_of = entry_group - seq_at
    reach_slot = jnp.where(reach_of < 0, reach_of + 2, reach_of + 1)
    reach_slot = jnp.clip(reach_slot, 0, len(REACH) - 1)
    entry_rank = near_rank[reach_slot, entry_local]
    local_lists = jnp.where(
        reach_of == 0, entry_local, group_tiles + NEAR * reach_slot + entry_rank
    )
    global_slots = group_tiles + NEAR * len(REACH) + jnp.arange(GLOBAL, dtype=jnp.int32)
    query_tiles = query.reshape(tile_count, TILE, feat_width)

    def per_tile(tile_args):
        query_tile, local_ids, live_count = tile_args
        slot_live_row = jnp.concatenate(
            [jnp.arange(KT) < live_count, jnp.ones((GLOBAL,), dtype=bool)]
        )
        key_live = jnp.repeat(slot_live_row, TILE)
        key_values = window[jnp.concatenate([local_ids, global_slots])].reshape(
            (KT + GLOBAL) * TILE, 2 * feat_width
        )
        return attend_tile(query_tile, key_values, key_live, feat_width)

    heads_out = lax.map(per_tile, (query_tiles, local_lists, kv_count)).reshape(
        tok_rows, feat_width
    )
    return jnp.dot(
        heads_out,
        lax.all_gather(w_out, "fsdp", axis=0, tiled=True),
        preferred_element_type=jnp.float32,
    ).astype(jnp.bfloat16)


def solution(mesh):
    return jax.shard_map(
        local,
        mesh=mesh,
        in_specs=(
            P(("seq", "fsdp"), None),
            P(("seq", "fsdp")),
            P(("seq", "fsdp"), None),
            P(("seq", "fsdp")),
            P(),
            P(),
            P(),
            P(),
            P(),
            P("fsdp", None),
            P("fsdp", None),
        ),
        out_specs=P(("seq", "fsdp"), None),
        check_vma=False,
    )
```

profile of v0, /device:TPU:88, one launch (start us, length us, event | category | flops | bytes accessed | tf_op | source)
XLA Modules:
  0.0 479.7 jit_solution(12287502584570003710)
XLA Ops:
  12.6 92.8 %all-gather.4.cloned.1.call-done = bf16[1280,3840]{1,0:T(8,128)(2,1)} async-done(((bf16[320,3840]{1,0:T(8,128)(2,1)}), bf16[1280,3840]{1,0:T(8,128)(2,1)}) %all-gather.4.cloned.1.call-update) | async-done | bytes 9830416 | tf_op jit(solution)/shard_map/all_gather | solution.py:108
  105.4 6.6 %convolution_convert_fusion = bf16[256,3840]{1,0:T(8,128)(2,1)S(1)} fusion(bf16[1280,3840]{1,0:T(8,128)(2,1)} %all-gather.4.cloned.1.call-done, bf16[256,1280]{1,0:T(8,128)(2,1)S(1)} %get-tuple-element.108, f32[1280]{0:T(1024)S(1)} %convert_element_type.133, f32[1280]{0:T(1024)S(1)} %convert_element_type.132, f32[256]{0:T(256)S(1)} %add_rsqrt_fusion, ...), kind=kOutput, calls=%fused_computation.34 | convolution fusion | flops 2519531520 | bytes 12464128 | tf_op jit(solution)/shard_map/dot_general | solution.py:110
  119.2 3.1 collective-permute-start.8
  123.8 13.3 %collective-permute-done.8 = bf16[2,128,1280]{2,1,0:T(8,128)(2,1)S(1)} collective-permute-done((bf16[2,128,1280]{2,1,0:T(8,128)(2,1)S(1)}, bf16[2,128,1280]{2,1,0:T(8,128)(2,1)S(1)}, u32[]{:S(2)}, u32[]{:S(2)}) %collective-permute-start.8) | collective-permute-done | bytes 655392 | tf_op jit(solution)/shard_map/ppermute | solution.py:102
  137.3 1.5 collective-permute-start.9
  139.3 13.6 %collective-permute-done.9 = bf16[2,128,1280]{2,1,0:T(8,128)(2,1)S(1)} collective-permute-done((bf16[2,128,1280]{2,1,0:T(8,128)(2,1)S(1)}, bf16[2,128,1280]{2,1,0:T(8,128)(2,1)S(1)}, u32[]{:S(2)}, u32[]{:S(2)}) %collective-permute-start.9) | collective-permute-done | bytes 655392 | tf_op jit(solution)/shard_map/ppermute | solution.py:102
  155.2 2.0 pad_add_fusion.1
  157.1 1.9 collective-permute-start
  160.0 2.0 pad_add_fusion.2
  161.9 1.9 collective-permute-start.2
  163.8 5.5 %collective-permute-done.10 = bf16[2,128,1280]{2,1,0:T(8,128)(2,1)S(1)} collective-permute-done((bf16[2,128,1280]{2,1,0:T(8,128)(2,1)S(1)}, bf16[2,128,1280]{2,1,0:T(8,128)(2,1)S(1)}, u32[]{:S(2)}, u32[]{:S(2)}) %collective-permute-start.10) | collective-permute-done | bytes 655392 | tf_op jit(solution)/shard_map/ppermute | solution.py:102
  171.2 2.0 pad_add_fusion.3
  173.2 1.9 collective-permute-start.4
  175.3 8.0 %collective-permute-done.11 = bf16[2,128,1280]{2,1,0:T(8,128)(2,1)S(1)} collective-permute-done((bf16[2,128,1280]{2,1,0:T(8,128)(2,1)S(1)}, bf16[2,128,1280]{2,1,0:T(8,128)(2,1)S(1)}, u32[]{:S(2)}, u32[]{:S(2)}) %collective-permute-start.11) | collective-permute-done | bytes 655392 | tf_op jit(solution)/shard_map/ppermute | solution.py:102
  184.2 2.0 pad_add_fusion.4
  186.2 3.9 collective-permute-start.6
  192.1 23.7 %collective-permute-done.13 = bf16[2,128,1280]{2,1,0:T(8,128)(2,1)S(1)} collective-permute-done((bf16[2,128,1280]{2,1,0:T(8,128)(2,1)S(1)}, bf16[2,128,1280]{2,1,0:T(8,128)(2,1)S(1)}, u32[]{:S(2)}, u32[]{:S(2)}) %collective-permute-start.13) | collective-permute-done | bytes 655392 | tf_op jit(solution)/shard_map/ppermute | solution.py:102
  216.1 30.4 %collective-permute-done.14 = bf16[2,128,1280]{2,1,0:T(8,128)(2,1)S(1)} collective-permute-done((bf16[2,128,1280]{2,1,0:T(8,128)(2,1)S(1)}, bf16[2,128,1280]{2,1,0:T(8,128)(2,1)S(1)}, u32[]{:S(2)}, u32[]{:S(2)}) %collective-permute-start.14) | collective-permute-done | bytes 655392 | tf_op jit(solution)/shard_map/ppermute | solution.py:102
  246.9 4.5 gather_fusion.4
  251.5 2.3 collective-permute-start.1
  254.1 4.5 gather_fusion.5
  258.6 1.9 collective-permute-start.3
  260.5 4.6 gather_fusion.6
  265.1 3.6 collective-permute-start.5
  269.1 4.7 gather_fusion.7
  273.8 4.0 collective-permute-start.7
  277.8 4.7 fusion.17
  282.8 16.5 %collective-permute-done.1 = bf16[3,128,2560]{2,1,0:T(8,128)(2,1)} collective-permute-done((bf16[3,128,2560]{2,1,0:T(8,128)(2,1)}, bf16[3,128,2560]{2,1,0:T(8,128)(2,1)}, u32[]{:S(2)}, u32[]{:S(2)}) %collective-permute-start.1) | collective-permute-done | bytes 1966112 | tf_op jit(solution)/shard_map/ppermute | solution.py:18
  299.3 1.7 constant_dynamic-update-slice_fusion.5
  301.0 15.2 %collective-permute-done.3 = bf16[3,128,2560]{2,1,0:T(8,128)(2,1)} collective-permute-done((bf16[3,128,2560]{2,1,0:T(8,128)(2,1)}, bf16[3,128,2560]{2,1,0:T(8,128)(2,1)}, u32[]{:S(2)}, u32[]{:S(2)}) %collective-permute-start.3) | collective-permute-done | bytes 1966112 | tf_op jit(solution)/shard_map/ppermute | solution.py:18
  316.3 1.7 constant_dynamic-update-slice_fusion.4
  317.9 1.7 constant_dynamic-update-slice_fusion.3
  319.7 17.5 %collective-permute-done.7 = bf16[3,128,2560]{2,1,0:T(8,128)(2,1)S(1)} collective-permute-done((bf16[3,128,2560]{2,1,0:T(8,128)(2,1)}, bf16[3,128,2560]{2,1,0:T(8,128)(2,1)S(1)}, u32[]{:S(2)}, u32[]{:S(2)}) %collective-permute-start.7) | collective-permute-done | bytes 1966112 | tf_op jit(solution)/shard_map/ppermute | solution.py:18
  337.5 5.0 %copy-done.2 = bf16[22,128,2560]{2,1,0:T(8,128)(2,1)} copy-done((bf16[22,128,2560]{2,1,0:T(8,128)(2,1)}, bf16[22,128,2560]{2,1,0:T(8,128)(2,1)S(1)}, u32[]{:S(2)}) %copy-start.2) | copy-done | bytes 14417944
  342.5 126.8 %while.11 = (s32[]{:T(128)}, bf16[2,128,1280]{2,1,0:T(8,128)(2,1)S(1)}, s32[2,16]{1,0:T(2,128)S(1)}, bf16[22,128,2560]{2,1,0:T(8,128)(2,1)}, s32[2]{0:T(128)S(1)...) while((s32[]{:T(128)}, bf16[2,128,1280]{2,1,0:T(8,128)(2,1)S(1)}, ...), condition=%wide.region_27.28_spmd.clone, body=%wide.region_24.27_spmd.clone.sunk | while | flops 1538428160 | bytes 123626584 | solution.py:154
  342.6 11.3 %gather_fusion = bf16[18,128,2560]{2,1,0:T(8,128)(2,1)} fusion(bf16[22,128,2560]{2,1,0:T(8,128)(2,1)} %get-tuple-element.203, s32[1024]{0:T(1024)S(1)} %pad_clamp_fusion.8), kind=kCustom, calls=%fused_computation.clone.clone.1 | custom fusion | bytes 23593032 | tf_op jit(solution)/shard_map/while/body/eval_jaxpr/gather | solution.py:149
  353.9 9.7 %fusion.97 = (bf16[2304,1280]{1,0:T(8,128)(2,1)}, bf16[2304,1280]{1,0:T(8,128)(2,1)}) fusion(bf16[2304,2560]{1,0:T(8,128)(2,1)} %bitcast.177), kind=kLoop, calls=%fused_computation.184.clone.1 | loop fusion | bytes 23592960 | tf_op jit(solution)/shard_map/while/body/eval_jaxpr/slice | solution.py:53
  363.5 8.9 %copy.34 = bf16[2304,1280]{0,1:T(8,128)(2,1)} copy(bf16[2304,1280]{1,0:T(8,128)(2,1)} %get-tuple-element.181) | data formatting | bytes 11796480 | tf_op jit(solution)/shard_map/while
  374.0 11.3 %fusion.98 = (f32[16,128]{1,0:T(8,128)S(1)}, f32[16,128,2304]{2,1,0:T(8,128)}) fusion(pred[2304]{0:T(1024)(128)(4,1)S(1)} %broadcast_bitcast_fusion.2, bf16[128,16,80]{0,2,1:T(8,128)(2,1)S(1)} %bitcast.187, bf16[2304,16,80]{0,2,1:T(8,128)(2,1)} %bitcast.178), kind=kOutput, calls=%fused_computation.185.clone.1 | convolution fusion | flops 773851392 | bytes 25110784 | tf_op jit(solution)/shard_map/while/body/eval_jaxpr/sub | solution.py:60
  385.3 8.9 %copy.32 = bf16[2304,1280]{0,1:T(8,128)(2,1)} copy(bf16[2304,1280]{1,0:T(8,128)(2,1)} %get-tuple-element.180) | data formatting | bytes 11796480 | tf_op jit(solution)/shard_map/while
  394.1 11.5 %fusion.99 = bf16[16,80,128]{2,1,0:T(8,128)(2,1)S(1)} fusion(bf16[2304,16,80]{0,2,1:T(8,128)(2,1)} %bitcast.179, f32[16,128,2304]{2,1,0:T(8,128)} %get-tuple-element.182, f32[16,128]{1,0:T(8,128)S(1)} %get-tuple-element.183), kind=kOutput, calls=%fused_computation.19.clone.1 | convolution fusion | flops 764575744 | bytes 25108480 | tf_op jit(solution)/shard_map/while/body/eval_jaxpr/hqk,khd->qhd/dot_general | solution.py:62
  406.0 11.3 %gather_fusion = bf16[18,128,2560]{2,1,0:T(8,128)(2,1)} fusion(bf16[22,128,2560]{2,1,0:T(8,128)(2,1)} %get-tuple-element.203, s32[1024]{0:T(1024)S(1)} %pad_clamp_fusion.8), kind=kCustom, calls=%fused_computation.clone.clone.1 | custom fusion | bytes 23593032 | tf_op jit(solution)/shard_map/while/body/eval_jaxpr/gather | solution.py:149
  417.3 9.7 %fusion.97 = (bf16[2304,1280]{1,0:T(8,128)(2,1)}, bf16[2304,1280]{1,0:T(8,128)(2,1)}) fusion(bf16[2304,2560]{1,0:T(8,128)(2,1)} %bitcast.177), kind=kLoop, calls=%fused_computation.184.clone.1 | loop fusion | bytes 23592960 | tf_op jit(solution)/shard_map/while/body/eval_jaxpr/slice | solution.py:53
  426.9 8.9 %copy.34 = bf16[2304,1280]{0,1:T(8,128)(2,1)} copy(bf16[2304,1280]{1,0:T(8,128)(2,1)} %get-tuple-element.181) | data formatting | bytes 11796480 | tf_op jit(solution)/shard_map/while
  437.4 11.3 %fusion.98 = (f32[16,128]{1,0:T(8,128)S(1)}, f32[16,128,2304]{2,1,0:T(8,128)}) fusion(pred[2304]{0:T(1024)(128)(4,1)S(1)} %broadcast_bitcast_fusion.2, bf16[128,16,80]{0,2,1:T(8,128)(2,1)S(1)} %bitcast.187, bf16[2304,16,80]{0,2,1:T(8,128)(2,1)} %bitcast.178), kind=kOutput, calls=%fused_computation.185.clone.1 | convolution fusion | flops 773851392 | bytes 25110784 | tf_op jit(solution)/shard_map/while/body/eval_jaxpr/sub | solution.py:60
  448.6 8.9 %copy.32 = bf16[2304,1280]{0,1:T(8,128)(2,1)} copy(bf16[2304,1280]{1,0:T(8,128)(2,1)} %get-tuple-element.180) | data formatting | bytes 11796480 | tf_op jit(solution)/shard_map/while
  457.5 11.5 %fusion.99 = bf16[16,80,128]{2,1,0:T(8,128)(2,1)S(1)} fusion(bf16[2304,16,80]{0,2,1:T(8,128)(2,1)} %bitcast.179, f32[16,128,2304]{2,1,0:T(8,128)} %get-tuple-element.182, f32[16,128]{1,0:T(8,128)S(1)} %get-tuple-element.183), kind=kOutput, calls=%fused_computation.19.clone.1 | convolution fusion | flops 764575744 | bytes 25108480 | tf_op jit(solution)/shard_map/while/body/eval_jaxpr/hqk,khd->qhd/dot_general | solution.py:62
  469.3 3.9 convolution_convert_fusion.1
  (132 shorter events, 23.7 us)
Async XLA Ops:
  6.5 4.1 copy-start
  6.5 2.8 copy-start.3
  6.5 98.9 %all-gather.4.cloned.1.call-start = ((), (), s32[]{:S(2)}) async-start(), calls=%async_computation | async-start | bytes 12288000 | tf_op jit(solution)/shard_map/all_gather | solution.py:108
  7.3 239.7 %all-gather.6.cloned.1.call-start = ((), (), s32[]{:S(2)}) async-start(), calls=%async_computation.1 | async-start | bytes 6553600 | tf_op jit(solution)/shard_map/all_gather | solution.py:119
  10.6 1.3 copy-start.5
  112.1 1.3 copy-start.4
  113.3 1.2 copy-start.7
  113.3 10.3 %copy-start.6 = (s32[2,16]{1,0:T(2,128)S(1)}, s32[2,16]{1,0:T(2,128)}, u32[]{:S(2)}) copy-start(s32[2,16]{1,0:T(2,128)} %param.15) | copy-start | bytes 388
  114.5 354.8 %all-gather.8.cloned.1.call-start = ((), (), s32[]{:S(2)}) async-start(), calls=%async_computation.2 | async-start | bytes 4096000 | tf_op jit(solution)/shard_map/all_gather | solution.py:159
  119.2 17.9 %collective-permute-start.8 = (bf16[2,128,1280]{2,1,0:T(8,128)(2,1)S(1)}, bf16[2,128,1280]{2,1,0:T(8,128)(2,1)S(1)}, u32[]{:S(2)}, u32[]{:S(2)}) collective-permute-start(bf16[2,128,1280]{2,1,0:T(8,128)(2,1)S(1)} %pad_maximum_fusion), channel_id=1, source_target_pairs={{0,64},{1,65},{2,66},{3,67},{4,68},{5,69},{6,70},{7,71},{8,72},{9,... | collective-permute-start | bytes 1966088 | tf_op jit(solution)/shard_map/ppermute | solution.py:102
  137.3 15.5 %collective-permute-start.9 = (bf16[2,128,1280]{2,1,0:T(8,128)(2,1)S(1)}, bf16[2,128,1280]{2,1,0:T(8,128)(2,1)S(1)}, u32[]{:S(2)}, u32[]{:S(2)}) collective-permute-start(bf16[2,128,1280]{2,1,0:T(8,128)(2,1)S(1)} %broadcast_select_fusion), channel_id=1, source_target_pairs={{0,32},{1,33},{2,34},{3,35},{4,36},{5,37},{6,38},{7,39},{8,40},{9,... | collective-permute-start | bytes 1966088 | tf_op jit(solution)/shard_map/ppermute | solution.py:102
  153.0 16.3 %collective-permute-start.10 = (bf16[2,128,1280]{2,1,0:T(8,128)(2,1)S(1)}, bf16[2,128,1280]{2,1,0:T(8,128)(2,1)S(1)}, u32[]{:S(2)}, u32[]{:S(2)}) collective-permute-start(bf16[2,128,1280]{2,1,0:T(8,128)(2,1)S(1)} %broadcast_select_fusion.1), channel_id=1, source_target_pairs={{0,16},{1,17},{2,18},{3,19},{4,20},{5,21},{6,22},{7,23},{8,24},{9,... | collective-permute-start | bytes 1966088 | tf_op jit(solution)/shard_map/ppermute | solution.py:102
  157.1 34.9 %collective-permute-start = (s32[3]{0:T(128)S(1)}, s32[3]{0:T(128)S(1)}, u32[]{:S(2)}, u32[]{:S(2)}) collective-permute-start(s32[3]{0:T(128)S(1)} %pad_add_fusion.1), channel_id=1, source_target_pairs={{8,0},{12,4},{16,8},{20,12},{24,16},{28,20},{32,24},{36,28},{40,32... | collective-permute-start | bytes 44 | tf_op jit(solution)/shard_map/ppermute | solution.py:18
  161.9 30.1 %collective-permute-start.2 = (s32[3]{0:T(128)S(1)}, s32[3]{0:T(128)S(1)}, u32[]{:S(2)}, u32[]{:S(2)}) collective-permute-start(s32[3]{0:T(128)S(1)} %pad_add_fusion.2), channel_id=1, source_target_pairs={{4,0},{8,4},{12,8},{16,12},{20,16},{24,20},{28,24},{32,28},{36,32}... | collective-permute-start | bytes 44 | tf_op jit(solution)/shard_map/ppermute | solution.py:18
  169.4 13.9 %collective-permute-start.11 = (bf16[2,128,1280]{2,1,0:T(8,128)(2,1)S(1)}, bf16[2,128,1280]{2,1,0:T(8,128)(2,1)S(1)}, u32[]{:S(2)}, u32[]{:S(2)}) collective-permute-start(bf16[2,128,1280]{2,1,0:T(8,128)(2,1)S(1)} %broadcast_select_fusion.2), channel_id=1, source_target_pairs={{0,8},{1,9},{2,10},{3,11},{4,12},{5,13},{6,14},{7,15},{8,0},{9,1},... | collective-permute-start | bytes 1966088 | tf_op jit(solution)/shard_map/ppermute | solution.py:102
  173.2 42.9 %collective-permute-start.4 = (s32[3]{0:T(128)S(1)}, s32[3]{0:T(128)S(1)}, u32[]{:S(2)}, u32[]{:S(2)}) collective-permute-start(s32[3]{0:T(128)S(1)} %pad_add_fusion.3), channel_id=1, source_target_pairs={{0,4},{4,8},{8,12},{12,16},{16,20},{20,24},{24,28},{28,32},{32,36}... | collective-permute-start | bytes 44 | tf_op jit(solution)/shard_map/ppermute | solution.py:18
  183.4 6.7 %collective-permute-start.12 = (bf16[2,128,1280]{2,1,0:T(8,128)(2,1)S(1)}, bf16[2,128,1280]{2,1,0:T(8,128)(2,1)S(1)}, u32[]{:S(2)}, u32[]{:S(2)}) collective-permute-start(bf16[2,128,1280]{2,1,0:T(8,128)(2,1)S(1)} %broadcast_select_fusion.3), channel_id=1, source_target_pairs={{0,4},{1,5},{2,6},{3,7},{4,0},{5,1},{6,2},{7,3},{8,12},{9,13},{10,... | collective-permute-start | bytes 1966088 | tf_op jit(solution)/shard_map/ppermute | solution.py:102
  186.2 29.9 %collective-permute-start.6 = (s32[3]{0:T(128)S(1)}, s32[3]{0:T(128)S(1)}, u32[]{:S(2)}, u32[]{:S(2)}) collective-permute-start(s32[3]{0:T(128)S(1)} %pad_add_fusion.4), channel_id=1, source_target_pairs={{0,8},{4,12},{8,16},{12,20},{16,24},{20,28},{24,32},{28,36},{32,40... | collective-permute-start | bytes 44 | tf_op jit(solution)/shard_map/ppermute | solution.py:18
  190.3 25.5 %collective-permute-start.13 = (bf16[2,128,1280]{2,1,0:T(8,128)(2,1)S(1)}, bf16[2,128,1280]{2,1,0:T(8,128)(2,1)S(1)}, u32[]{:S(2)}, u32[]{:S(2)}) collective-permute-start(bf16[2,128,1280]{2,1,0:T(8,128)(2,1)S(1)} %broadcast_select_fusion.4), channel_id=1, source_target_pairs={{0,2},{1,3},{2,0},{3,1},{4,6},{5,7},{6,4},{7,5},{8,10},{9,11},{10,... | collective-permute-start | bytes 1966088 | tf_op jit(solution)/shard_map/ppermute | solution.py:102
  216.0 30.6 %collective-permute-start.14 = (bf16[2,128,1280]{2,1,0:T(8,128)(2,1)S(1)}, bf16[2,128,1280]{2,1,0:T(8,128)(2,1)S(1)}, u32[]{:S(2)}, u32[]{:S(2)}) collective-permute-start(bf16[2,128,1280]{2,1,0:T(8,128)(2,1)S(1)} %broadcast_select_fusion.5), channel_id=1, source_target_pairs={{0,1},{1,0},{2,3},{3,2},{4,5},{5,4},{6,7},{7,6},{8,9},{9,8},{10,11... | collective-permute-start | bytes 1966088 | tf_op jit(solution)/shard_map/ppermute | solution.py:102
  251.5 47.9 %collective-permute-start.1 = (bf16[3,128,2560]{2,1,0:T(8,128)(2,1)}, bf16[3,128,2560]{2,1,0:T(8,128)(2,1)}, u32[]{:S(2)}, u32[]{:S(2)}) collective-permute-start(bf16[3,128,2560]{2,1,0:T(8,128)(2,1)} %gather_fusion.4), channel_id=1, source_target_pairs={{0,8},{4,12},{8,16},{12,20},{16,24},{20,28},{24,32},{28,36},{32,40... | collective-permute-start | bytes 5898248 | tf_op jit(solution)/shard_map/ppermute | solution.py:18
  258.6 57.7 %collective-permute-start.3 = (bf16[3,128,2560]{2,1,0:T(8,128)(2,1)}, bf16[3,128,2560]{2,1,0:T(8,128)(2,1)}, u32[]{:S(2)}, u32[]{:S(2)}) collective-permute-start(bf16[3,128,2560]{2,1,0:T(8,128)(2,1)} %gather_fusion.5), channel_id=1, source_target_pairs={{0,4},{4,8},{8,12},{12,16},{16,20},{20,24},{24,28},{28,32},{32,36}... | collective-permute-start | bytes 5898248 | tf_op jit(solution)/shard_map/ppermute | solution.py:18
  265.1 52.9 %collective-permute-start.5 = (bf16[3,128,2560]{2,1,0:T(8,128)(2,1)}, bf16[3,128,2560]{2,1,0:T(8,128)(2,1)}, u32[]{:S(2)}, u32[]{:S(2)}) collective-permute-start(bf16[3,128,2560]{2,1,0:T(8,128)(2,1)} %gather_fusion.6), channel_id=1, source_target_pairs={{4,0},{8,4},{12,8},{16,12},{20,16},{24,20},{28,24},{32,28},{36,32}... | collective-permute-start | bytes 5898248 | tf_op jit(solution)/shard_map/ppermute | solution.py:18
  269.1 13.4 %slice-start = ((s8[5242880]{0:T(1024)(128)(4,1)}), s8[1048576]{0:T(1024)(128)(4,1)S(1)}, s32[]{:S(2)}) async-start(s8[5242880]{0:T(1024)(128)(4,1)} %bitcast.184), calls=%async_computation.3 | async-start | bytes 2097152
  273.7 8.7 %slice-start.1 = ((s8[5242880]{0:T(1024)(128)(4,1)}), s8[4194304]{0:T(1024)(128)(4,1)S(1)}, s32[]{:S(2)}) async-start(s8[5242880]{0:T(1024)(128)(4,1)} %bitcast.184), calls=%async_computation.4 | async-start | bytes 8388608
  273.8 63.5 %collective-permute-start.7 = (bf16[3,128,2560]{2,1,0:T(8,128)(2,1)}, bf16[3,128,2560]{2,1,0:T(8,128)(2,1)S(1)}, u32[]{:S(2)}, u32[]{:S(2)}) collective-permute-start(bf16[3,128,2560]{2,1,0:T(8,128)(2,1)} %gather_fusion.7), channel_id=1, source_target_pairs={{8,0},{12,4},{16,8},{20,12},{24,16},{28,20},{32,24},{36,28},{40,32... | collective-permute-start | bytes 5898248 | tf_op jit(solution)/shard_map/ppermute | solution.py:18
  319.6 22.9 %slice-start.2 = ((bf16[256,3840]{1,0:T(8,128)(2,1)}), bf16[256,1280]{1,0:T(8,128)(2,1)S(1)}, s32[]{:S(2)}) async-start(bf16[256,3840]{1,0:T(8,128)(2,1)} %copy-done.4), calls=%async_computation.5 | async-start | bytes 1310720 | tf_op jit(solution)/shard_map/slice | solution.py:111
  319.6 22.9 %copy-start.8 = (bf16[2,128,1280]{2,1,0:T(8,128)(2,1)S(1)}, bf16[2,128,1280]{2,1,0:T(8,128)(2,1)}, u32[]{:S(2)}) copy-start(bf16[2,128,1280]{2,1,0:T(8,128)(2,1)} %custom-call.17) | copy-start | bytes 1966084
  319.6 22.9 %copy-start.9 = (s32[2]{0:T(128)S(1)}, s32[2]{0:T(128)}, u32[]{:S(2)}) copy-start(s32[2]{0:T(128)} %param.16) | copy-start | bytes 28
  337.5 5.0 %copy-start.2 = (bf16[22,128,2560]{2,1,0:T(8,128)(2,1)}, bf16[22,128,2560]{2,1,0:T(8,128)(2,1)S(1)}, u32[]{:S(2)}) copy-start(bf16[22,128,2560]{2,1,0:T(8,128)(2,1)S(1)} %constant_dynamic-update-slice_fusion.1) | copy-start | bytes 43253764
  469.3 3.9 copy-start.1
Sparse Core Ops, SparseCore 0:
  9.0 96.3 all-gather.3
  114.6 57.4 all-gather.5
  190.3 58.4 all-gather.7
where the time goes:
time: 481 us; the launch traced here: 480 us
  waiting for transfers between devices  237 us (49%)
  local copies, waits for them, and re-layouts  115 us (24%)
  matrix products  60.9 us (13%)
  starting transfers between devices  29.4 us (6%)
  between operations  18.8 us (4%)
  other arithmetic  17.9 us (4%)
    ppermute x7, waiting for transfers between devices, local(): lax.ppermute(global_stream, ('seq', 'fsdp'), [(i, i ^ step) for i in rang...  94.5 us
    all_gather x1, waiting for transfers between devices, local(): w_full = lax.all_gather(w_qkv, 'fsdp', axis=0, tiled=True)  92.8 us
    ppermute x8, waiting for transfers between devices, passed_along(): return lax.ppermute(block, axis, route)  49.3 us
    while x4, local copies, waits for them, and re-layouts  35.4 us
    dot_general x2, matrix products, attend_tile(): jnp.einsum('hqk,khd->qhd', probs, values_h, preferred_element_type=jnp.fl...  23.1 us
    sub x2, matrix products, attend_tile(): weights_raw = jnp.exp(scores - row_max)  22.6 us
    gather x2, local copies, waits for them, and re-layouts, per_tile(): window[jnp.concatenate([local_ids, global_slots])]  22.5 us
    ppermute x8, starting transfers between devices, passed_along(): return lax.ppermute(block, axis, route)  21.4 us
  transfers between devices with their start and end apart: 18, of which 10 were waited for; matrix products, arithmetic and copies ran while one was open for 37% of the time, Pallas kernels for 0%

commit v1 on v0

--- a/solution.py
+++ b/solution.py
@@ -105,7 +105,10 @@
         global_stream = jnp.where(held[:, None, None], global_stream, got)
         done_bits |= step
     global_stream = global_stream.reshape(GLOBAL * TILE, feat_width)
-    w_full = lax.all_gather(w_qkv, "fsdp", axis=0, tiled=True)
+    block_last = tuple((w_qkv for _ in range(lax.axis_size("fsdp"))))
+    part_next = jnp.stack(block_last, axis=0)
+    small = lax.all_to_all(part_next, "fsdp", 0, 0)
+    w_full = jnp.concatenate(small, 0)
     normed = layer_norm(stream, ln_gain, ln_bias)
     qkv = jnp.dot(normed, w_full, preferred_element_type=jnp.float32).astype(jnp.bfloat16)
     query = qkv[:, :feat_width]

time: 481 us -> 502 us (1.044)
  starting transfers between devices: 29.4 us -> 42.3 us
  local copies, waits for them, and re-layouts: 115 us -> 121 us
    all_to_all x0 -> x1, waiting for transfers between devices: none -> 103 us  [local(): small = lax.all_to_all(part_next, 'fsdp', 0, 0)]
    all_gather x1 -> x0, waiting for transfers between devices: 92.8 us -> none  [local(): w_full = lax.all_gather(w_qkv, 'fsdp', axis=0, tiled=True)]
    ppermute x7, waiting for transfers between devices: 94.5 us -> 85.7 us  [local(): lax.ppermute(global_stream, ('seq', 'fsdp'), [(i, i ^ step) for i in rang...]
    another operation x0 -> x1, local copies, waits for them, and re-layouts: none -> 6.2 us  [local(): part_next = jnp.stack(block_last, axis=0)]
    all_to_all x0 -> x1, starting transfers between devices: none -> 6.04 us  [local(): small = lax.all_to_all(part_next, 'fsdp', 0, 0)]
    unnamed x29 -> x35, local copies, waits for them, and re-layouts: 11.8 us -> 11.8 us
  transfers between devices with their start and end apart: 18 -> 18, of which waited for: 10 -> 10; matrix products, arithmetic and copies ran while one was open for 37% -> 35% of each run, Pallas kernels for 0% -> 0%
where the time goes in v1:
time: 502 us; the launch traced here: 497 us
  waiting for transfers between devices  237 us (47%)
  local copies, waits for them, and re-layouts  121 us (24%)
  matrix products  60.9 us (12%)
  starting transfers between devices  42.3 us (8%)
  between operations  19.2 us (4%)
  other arithmetic  15.9 us (3%)
    all_to_all x1, waiting for transfers between devices, local(): small = lax.all_to_all(part_next, 'fsdp', 0, 0)  103 us
    ppermute x7, waiting for transfers between devices, local(): lax.ppermute(global_stream, ('seq', 'fsdp'), [(i, i ^ step) for i in rang...  85.7 us
    ppermute x8, waiting for transfers between devices, passed_along(): return lax.ppermute(block, axis, route)  48.3 us
    while x4, local copies, waits for them, and re-layouts  35.4 us
    ppermute x8, starting transfers between devices, passed_along(): return lax.ppermute(block, axis, route)  23.4 us
    dot_general x2, matrix products, attend_tile(): jnp.einsum('hqk,khd->qhd', probs, values_h, preferred_element_type=jnp.fl...  23.1 us
    sub x2, matrix products, attend_tile(): weights_raw = jnp.exp(scores - row_max)  22.6 us
    gather x2, local copies, waits for them, and re-layouts, per_tile(): window[jnp.concatenate([local_ids, global_slots])]  22.5 us
  transfers between devices with their start and end apart: 18, of which 10 were waited for; matrix products, arithmetic and copies ran while one was open for 35% of the time, Pallas kernels for 0%

profile of v1, /device:TPU:88, one launch (start us, length us, event | category | flops | bytes accessed | tf_op | source)
XLA Modules:
  0.0 496.7 jit_solution(8497161101955536673)
XLA Ops:
  6.5 6.2 %stack.81 = bf16[4,320,3840]{2,1,0:T(8,128)(2,1)} broadcast(bf16[320,3840]{1,0:T(8,128)(2,1)} %param.22), dimensions={1,2} | broadcast | bytes 12288000 | tf_op jit(solution)/shard_map/stack | solution.py:109
  12.7 6.0 %all-to-all-start = ((bf16[4,320,3840]{2,1,0:T(8,128)(2,1)}), bf16[4,320,3840]{2,1,0:T(8,128)(2,1)}, u32[]{:S(2)}, u32[]{:S(2)}) async-start(bf16[4,320,3840]{2,1,0:T(8,128)(2,1)} %stack.81), calls=%async_computation | async-start | bytes 19660800 | tf_op jit(solution)/shard_map/all_to_all | solution.py:110
  22.2 103.0 %all-to-all-done = bf16[4,320,3840]{2,1,0:T(8,128)(2,1)} async-done(((bf16[4,320,3840]{2,1,0:T(8,128)(2,1)}), bf16[4,320,3840]{2,1,0:T(8,128)(2,1)}, u32[]{:S(2)}, u32[]{:S(2)}) %all-to-all-start) | async-done | bytes 9830432 | tf_op jit(solution)/shard_map/all_to_all | solution.py:110
  125.2 6.6 %convolution_convert_fusion = bf16[256,3840]{1,0:T(8,128)(2,1)S(1)} fusion(bf16[1280,3840]{1,0:T(8,128)(2,1)} %bitcast.8, bf16[256,1280]{1,0:T(8,128)(2,1)S(1)} %get-tuple-element.108, f32[1280]{0:T(1024)S(1)} %convert_element_type.133, f32[1280]{0:T(1024)S(1)} %convert_element_type.132, f32[256]{0:T(256)S(1)} %add_rsqrt_fusion, ...), kind=kOutput, calls=%fused_computation.34 | convolution fusion | flops 2519531520 | bytes 12464128 | tf_op jit(solution)/shard_map/dot_general | solution.py:113
  139.0 3.1 collective-permute-start.8
  143.6 12.5 %collective-permute-done.8 = bf16[2,128,1280]{2,1,0:T(8,128)(2,1)S(1)} collective-permute-done((bf16[2,128,1280]{2,1,0:T(8,128)(2,1)S(1)}, bf16[2,128,1280]{2,1,0:T(8,128)(2,1)S(1)}, u32[]{:S(2)}, u32[]{:S(2)}) %collective-permute-start.8) | collective-permute-done | bytes 655392 | tf_op jit(solution)/shard_map/ppermute | solution.py:102
  158.2 12.7 %collective-permute-done.9 = bf16[2,128,1280]{2,1,0:T(8,128)(2,1)S(1)} collective-permute-done((bf16[2,128,1280]{2,1,0:T(8,128)(2,1)S(1)}, bf16[2,128,1280]{2,1,0:T(8,128)(2,1)S(1)}, u32[]{:S(2)}, u32[]{:S(2)}) %collective-permute-start.9) | collective-permute-done | bytes 655392 | tf_op jit(solution)/shard_map/ppermute | solution.py:102
  173.1 2.0 pad_add_fusion.1
  175.1 2.5 collective-permute-start
  178.5 2.0 pad_add_fusion.2
  180.5 1.9 collective-permute-start.2
  182.4 4.2 collective-permute-done.10
  188.5 2.0 pad_add_fusion.3
  190.4 1.9 collective-permute-start.4
  192.5 7.3 %collective-permute-done.11 = bf16[2,128,1280]{2,1,0:T(8,128)(2,1)S(1)} collective-permute-done((bf16[2,128,1280]{2,1,0:T(8,128)(2,1)S(1)}, bf16[2,128,1280]{2,1,0:T(8,128)(2,1)S(1)}, u32[]{:S(2)}, u32[]{:S(2)}) %collective-permute-start.11) | collective-permute-done | bytes 655392 | tf_op jit(solution)/shard_map/ppermute | solution.py:102
  200.8 2.0 pad_add_fusion.4
  202.8 5.3 %collective-permute-start.6 = (s32[3]{0:T(128)S(1)}, s32[3]{0:T(128)S(1)}, u32[]{:S(2)}, u32[]{:S(2)}) collective-permute-start(s32[3]{0:T(128)S(1)} %pad_add_fusion.4), channel_id=1, source_target_pairs={{0,8},{4,12},{8,16},{12,20},{16,24},{20,28},{24,32},{28,36},{32,40... | collective-permute-start | bytes 44 | tf_op jit(solution)/shard_map/ppermute | solution.py:18
  208.3 4.2 collective-permute-start.13
  213.5 19.6 %collective-permute-done.13 = bf16[2,128,1280]{2,1,0:T(8,128)(2,1)S(1)} collective-permute-done((bf16[2,128,1280]{2,1,0:T(8,128)(2,1)S(1)}, bf16[2,128,1280]{2,1,0:T(8,128)(2,1)S(1)}, u32[]{:S(2)}, u32[]{:S(2)}) %collective-permute-start.13) | collective-permute-done | bytes 655392 | tf_op jit(solution)/shard_map/ppermute | solution.py:102
  234.9 29.4 %collective-permute-done.14 = bf16[2,128,1280]{2,1,0:T(8,128)(2,1)S(1)} collective-permute-done((bf16[2,128,1280]{2,1,0:T(8,128)(2,1)S(1)}, bf16[2,128,1280]{2,1,0:T(8,128)(2,1)S(1)}, u32[]{:S(2)}, u32[]{:S(2)}) %collective-permute-start.14) | collective-permute-done | bytes 655392 | tf_op jit(solution)/shard_map/ppermute | solution.py:102
  264.6 4.5 gather_fusion.4
  269.1 2.7 collective-permute-start.1
  272.2 4.5 gather_fusion.5
  276.7 1.9 collective-permute-start.3
  278.6 4.6 gather_fusion.6
  283.2 3.8 collective-permute-start.5
  287.3 4.7 gather_fusion.7
  292.0 3.4 collective-permute-start.7
  295.4 4.7 fusion.17
  300.5 16.5 %collective-permute-done.1 = bf16[3,128,2560]{2,1,0:T(8,128)(2,1)} collective-permute-done((bf16[3,128,2560]{2,1,0:T(8,128)(2,1)}, bf16[3,128,2560]{2,1,0:T(8,128)(2,1)}, u32[]{:S(2)}, u32[]{:S(2)}) %collective-permute-start.1) | collective-permute-done | bytes 1966112 | tf_op jit(solution)/shard_map/ppermute | solution.py:18
  318.7 16.5 %collective-permute-done.3 = bf16[3,128,2560]{2,1,0:T(8,128)(2,1)} collective-permute-done((bf16[3,128,2560]{2,1,0:T(8,128)(2,1)}, bf16[3,128,2560]{2,1,0:T(8,128)(2,1)}, u32[]{:S(2)}, u32[]{:S(2)}) %collective-permute-start.3) | collective-permute-done | bytes 1966112 | tf_op jit(solution)/shard_map/ppermute | solution.py:18
  336.9 1.7 constant_dynamic-update-slice_fusion.3
  338.6 15.3 %collective-permute-done.7 = bf16[3,128,2560]{2,1,0:T(8,128)(2,1)S(1)} collective-permute-done((bf16[3,128,2560]{2,1,0:T(8,128)(2,1)}, bf16[3,128,2560]{2,1,0:T(8,128)(2,1)S(1)}, u32[]{:S(2)}, u32[]{:S(2)}) %collective-permute-start.7) | collective-permute-done | bytes 1966112 | tf_op jit(solution)/shard_map/ppermute | solution.py:18
  354.1 5.0 %copy-done.2 = bf16[22,128,2560]{2,1,0:T(8,128)(2,1)} copy-done((bf16[22,128,2560]{2,1,0:T(8,128)(2,1)}, bf16[22,128,2560]{2,1,0:T(8,128)(2,1)S(1)}, u32[]{:S(2)}) %copy-start.2) | copy-done | bytes 14417944
  359.2 126.8 %while.11 = (s32[]{:T(128)}, bf16[2,128,1280]{2,1,0:T(8,128)(2,1)S(1)}, s32[2,16]{1,0:T(2,128)S(1)}, bf16[22,128,2560]{2,1,0:T(8,128)(2,1)}, s32[2]{0:T(128)S(1)...) while((s32[]{:T(128)}, bf16[2,128,1280]{2,1,0:T(8,128)(2,1)S(1)}, ...), condition=%wide.region_27.28_spmd.clone, body=%wide.region_24.27_spmd.clone.sunk | while | flops 1538428160 | bytes 123626584 | solution.py:157
  359.3 11.3 %gather_fusion = bf16[18,128,2560]{2,1,0:T(8,128)(2,1)} fusion(bf16[22,128,2560]{2,1,0:T(8,128)(2,1)} %get-tuple-element.203, s32[1024]{0:T(1024)S(1)} %pad_clamp_fusion.8), kind=kCustom, calls=%fused_computation.clone.clone.1 | custom fusion | bytes 23593032 | tf_op jit(solution)/shard_map/while/body/eval_jaxpr/gather | solution.py:152
  370.6 9.7 %fusion.97 = (bf16[2304,1280]{1,0:T(8,128)(2,1)}, bf16[2304,1280]{1,0:T(8,128)(2,1)}) fusion(bf16[2304,2560]{1,0:T(8,128)(2,1)} %bitcast.178), kind=kLoop, calls=%fused_computation.184.clone.1 | loop fusion | bytes 23592960 | tf_op jit(solution)/shard_map/while/body/eval_jaxpr/slice | solution.py:53
  380.2 8.9 %copy.34 = bf16[2304,1280]{0,1:T(8,128)(2,1)} copy(bf16[2304,1280]{1,0:T(8,128)(2,1)} %get-tuple-element.181) | data formatting | bytes 11796480 | tf_op jit(solution)/shard_map/while
  390.6 11.3 %fusion.98 = (f32[16,128]{1,0:T(8,128)S(1)}, f32[16,128,2304]{2,1,0:T(8,128)}) fusion(pred[2304]{0:T(1024)(128)(4,1)S(1)} %broadcast_bitcast_fusion.2, bf16[128,16,80]{0,2,1:T(8,128)(2,1)S(1)} %bitcast.188, bf16[2304,16,80]{0,2,1:T(8,128)(2,1)} %bitcast.179), kind=kOutput, calls=%fused_computation.185.clone.1 | convolution fusion | flops 773851392 | bytes 25110784 | tf_op jit(solution)/shard_map/while/body/eval_jaxpr/sub | solution.py:60
  401.9 8.9 %copy.32 = bf16[2304,1280]{0,1:T(8,128)(2,1)} copy(bf16[2304,1280]{1,0:T(8,128)(2,1)} %get-tuple-element.180) | data formatting | bytes 11796480 | tf_op jit(solution)/shard_map/while
  410.8 11.5 %fusion.99 = bf16[16,80,128]{2,1,0:T(8,128)(2,1)S(1)} fusion(bf16[2304,16,80]{0,2,1:T(8,128)(2,1)} %bitcast.180, f32[16,128,2304]{2,1,0:T(8,128)} %get-tuple-element.182, f32[16,128]{1,0:T(8,128)S(1)} %get-tuple-element.183), kind=kOutput, calls=%fused_computation.19.clone.1 | convolution fusion | flops 764575744 | bytes 25108480 | tf_op jit(solution)/shard_map/while/body/eval_jaxpr/hqk,khd->qhd/dot_general | solution.py:62
  422.7 11.3 %gather_fusion = bf16[18,128,2560]{2,1,0:T(8,128)(2,1)} fusion(bf16[22,128,2560]{2,1,0:T(8,128)(2,1)} %get-tuple-element.203, s32[1024]{0:T(1024)S(1)} %pad_clamp_fusion.8), kind=kCustom, calls=%fused_computation.clone.clone.1 | custom fusion | bytes 23593032 | tf_op jit(solution)/shard_map/while/body/eval_jaxpr/gather | solution.py:152
  433.9 9.7 %fusion.97 = (bf16[2304,1280]{1,0:T(8,128)(2,1)}, bf16[2304,1280]{1,0:T(8,128)(2,1)}) fusion(bf16[2304,2560]{1,0:T(8,128)(2,1)} %bitcast.178), kind=kLoop, calls=%fused_computation.184.clone.1 | loop fusion | bytes 23592960 | tf_op jit(solution)/shard_map/while/body/eval_jaxpr/slice | solution.py:53
  443.6 8.9 %copy.34 = bf16[2304,1280]{0,1:T(8,128)(2,1)} copy(bf16[2304,1280]{1,0:T(8,128)(2,1)} %get-tuple-element.181) | data formatting | bytes 11796480 | tf_op jit(solution)/shard_map/while
  454.0 11.3 %fusion.98 = (f32[16,128]{1,0:T(8,128)S(1)}, f32[16,128,2304]{2,1,0:T(8,128)}) fusion(pred[2304]{0:T(1024)(128)(4,1)S(1)} %broadcast_bitcast_fusion.2, bf16[128,16,80]{0,2,1:T(8,128)(2,1)S(1)} %bitcast.188, bf16[2304,16,80]{0,2,1:T(8,128)(2,1)} %bitcast.179), kind=kOutput, calls=%fused_computation.185.clone.1 | convolution fusion | flops 773851392 | bytes 25110784 | tf_op jit(solution)/shard_map/while/body/eval_jaxpr/sub | solution.py:60
  465.3 8.9 %copy.32 = bf16[2304,1280]{0,1:T(8,128)(2,1)} copy(bf16[2304,1280]{1,0:T(8,128)(2,1)} %get-tuple-element.180) | data formatting | bytes 11796480 | tf_op jit(solution)/shard_map/while
  474.2 11.5 %fusion.99 = bf16[16,80,128]{2,1,0:T(8,128)(2,1)S(1)} fusion(bf16[2304,16,80]{0,2,1:T(8,128)(2,1)} %bitcast.180, f32[16,128,2304]{2,1,0:T(8,128)} %get-tuple-element.182, f32[16,128]{1,0:T(8,128)S(1)} %get-tuple-element.183), kind=kOutput, calls=%fused_computation.19.clone.1 | convolution fusion | flops 764575744 | bytes 25108480 | tf_op jit(solution)/shard_map/while/body/eval_jaxpr/hqk,khd->qhd/dot_general | solution.py:62
  486.0 3.9 convolution_convert_fusion.1
  (138 shorter events, 26.4 us)
Async XLA Ops:
  6.5 13.7 %copy-start = (bf16[512,1280]{1,0:T(8,128)(2,1)S(1)}, bf16[512,1280]{1,0:T(8,128)(2,1)}, u32[]{:S(2)}) copy-start(bf16[512,1280]{1,0:T(8,128)(2,1)} %param.19) | copy-start | bytes 3932164
  12.7 6.1 %copy-start.6 = (bf16[1280]{0:T(1024)(128)(2,1)S(1)}, bf16[1280]{0:T(1024)(128)(2,1)}, u32[]{:S(2)}) copy-start(bf16[1280]{0:T(1024)(128)(2,1)} %param.20) | copy-start | bytes 7684
  12.7 6.1 %copy-start.7 = (bf16[1280]{0:T(1024)(128)(2,1)S(1)}, bf16[1280]{0:T(1024)(128)(2,1)}, u32[]{:S(2)}) copy-start(bf16[1280]{0:T(1024)(128)(2,1)} %param.21) | copy-start | bytes 7684
  12.7 6.1 %copy-start.10 = (s32[256]{0:T(256)S(1)}, s32[256]{0:T(256)}, u32[]{:S(2)}) copy-start(s32[256]{0:T(256)} %param.14) | copy-start | bytes 3076
  12.7 6.2 %copy-start.3 = (bf16[256,1280]{1,0:T(8,128)(2,1)S(1)}, bf16[256,1280]{1,0:T(8,128)(2,1)}, u32[]{:S(2)}) copy-start(bf16[256,1280]{1,0:T(8,128)(2,1)} %param.18) | copy-start | bytes 1966084
  12.7 112.4 %all-to-all-start = ((bf16[4,320,3840]{2,1,0:T(8,128)(2,1)}), bf16[4,320,3840]{2,1,0:T(8,128)(2,1)}, u32[]{:S(2)}, u32[]{:S(2)}) async-start(bf16[4,320,3840]{2,1,0:T(8,128)(2,1)} %stack.81), calls=%async_computation | async-start | bytes 19660800 | tf_op jit(solution)/shard_map/all_to_all | solution.py:110
  18.8 245.8 %all-gather.3.cloned.1.call-start = ((), (), s32[]{:S(2)}) async-start(), calls=%async_computation.1 | async-start | bytes 6553600 | tf_op jit(solution)/shard_map/all_gather | solution.py:122
  20.2 1.3 copy-start.5
  131.8 1.3 copy-start.4
  133.1 1.2 copy-start.9
  133.1 10.3 %copy-start.8 = (s32[2,16]{1,0:T(2,128)S(1)}, s32[2,16]{1,0:T(2,128)}, u32[]{:S(2)}) copy-start(s32[2,16]{1,0:T(2,128)} %param.15) | copy-start | bytes 388
  134.2 351.7 %all-gather.5.cloned.1.call-start = ((), (), s32[]{:S(2)}) async-start(), calls=%async_computation.2 | async-start | bytes 4096000 | tf_op jit(solution)/shard_map/all_gather | solution.py:162
  139.0 17.1 %collective-permute-start.8 = (bf16[2,128,1280]{2,1,0:T(8,128)(2,1)S(1)}, bf16[2,128,1280]{2,1,0:T(8,128)(2,1)S(1)}, u32[]{:S(2)}, u32[]{:S(2)}) collective-permute-start(bf16[2,128,1280]{2,1,0:T(8,128)(2,1)S(1)} %pad_maximum_fusion), channel_id=1, source_target_pairs={{0,64},{1,65},{2,66},{3,67},{4,68},{5,69},{6,70},{7,71},{8,72},{9,... | collective-permute-start | bytes 1966088 | tf_op jit(solution)/shard_map/ppermute | solution.py:102
  156.2 14.7 %collective-permute-start.9 = (bf16[2,128,1280]{2,1,0:T(8,128)(2,1)S(1)}, bf16[2,128,1280]{2,1,0:T(8,128)(2,1)S(1)}, u32[]{:S(2)}, u32[]{:S(2)}) collective-permute-start(bf16[2,128,1280]{2,1,0:T(8,128)(2,1)S(1)} %broadcast_select_fusion), channel_id=1, source_target_pairs={{0,32},{1,33},{2,34},{3,35},{4,36},{5,37},{6,38},{7,39},{8,40},{9,... | collective-permute-start | bytes 1966088 | tf_op jit(solution)/shard_map/ppermute | solution.py:102
  171.1 15.5 %collective-permute-start.10 = (bf16[2,128,1280]{2,1,0:T(8,128)(2,1)S(1)}, bf16[2,128,1280]{2,1,0:T(8,128)(2,1)S(1)}, u32[]{:S(2)}, u32[]{:S(2)}) collective-permute-start(bf16[2,128,1280]{2,1,0:T(8,128)(2,1)S(1)} %broadcast_select_fusion.1), channel_id=1, source_target_pairs={{0,16},{1,17},{2,18},{3,19},{4,20},{5,21},{6,22},{7,23},{8,24},{9,... | collective-permute-start | bytes 1966088 | tf_op jit(solution)/shard_map/ppermute | solution.py:102
  175.1 38.4 %collective-permute-start = (s32[3]{0:T(128)S(1)}, s32[3]{0:T(128)S(1)}, u32[]{:S(2)}, u32[]{:S(2)}) collective-permute-start(s32[3]{0:T(128)S(1)} %pad_add_fusion.1), channel_id=1, source_target_pairs={{8,0},{12,4},{16,8},{20,12},{24,16},{28,20},{32,24},{36,28},{40,32... | collective-permute-start | bytes 44 | tf_op jit(solution)/shard_map/ppermute | solution.py:18
  180.5 33.0 %collective-permute-start.2 = (s32[3]{0:T(128)S(1)}, s32[3]{0:T(128)S(1)}, u32[]{:S(2)}, u32[]{:S(2)}) collective-permute-start(s32[3]{0:T(128)S(1)} %pad_add_fusion.2), channel_id=1, source_target_pairs={{4,0},{8,4},{12,8},{16,12},{20,16},{24,20},{28,24},{32,28},{36,32}... | collective-permute-start | bytes 44 | tf_op jit(solution)/shard_map/ppermute | solution.py:18
  186.7 13.1 %collective-permute-start.11 = (bf16[2,128,1280]{2,1,0:T(8,128)(2,1)S(1)}, bf16[2,128,1280]{2,1,0:T(8,128)(2,1)S(1)}, u32[]{:S(2)}, u32[]{:S(2)}) collective-permute-start(bf16[2,128,1280]{2,1,0:T(8,128)(2,1)S(1)} %broadcast_select_fusion.2), channel_id=1, source_target_pairs={{0,8},{1,9},{2,10},{3,11},{4,12},{5,13},{6,14},{7,15},{8,0},{9,1},... | collective-permute-start | bytes 1966088 | tf_op jit(solution)/shard_map/ppermute | solution.py:102
  190.4 44.4 %collective-permute-start.4 = (s32[3]{0:T(128)S(1)}, s32[3]{0:T(128)S(1)}, u32[]{:S(2)}, u32[]{:S(2)}) collective-permute-start(s32[3]{0:T(128)S(1)} %pad_add_fusion.3), channel_id=1, source_target_pairs={{0,4},{4,8},{8,12},{12,16},{16,20},{20,24},{24,28},{28,32},{32,36}... | collective-permute-start | bytes 44 | tf_op jit(solution)/shard_map/ppermute | solution.py:18
  200.0 8.1 %collective-permute-start.12 = (bf16[2,128,1280]{2,1,0:T(8,128)(2,1)S(1)}, bf16[2,128,1280]{2,1,0:T(8,128)(2,1)S(1)}, u32[]{:S(2)}, u32[]{:S(2)}) collective-permute-start(bf16[2,128,1280]{2,1,0:T(8,128)(2,1)S(1)} %broadcast_select_fusion.3), channel_id=1, source_target_pairs={{0,4},{1,5},{2,6},{3,7},{4,0},{5,1},{6,2},{7,3},{8,12},{9,13},{10,... | collective-permute-start | bytes 1966088 | tf_op jit(solution)/shard_map/ppermute | solution.py:102
  202.8 32.1 %collective-permute-start.6 = (s32[3]{0:T(128)S(1)}, s32[3]{0:T(128)S(1)}, u32[]{:S(2)}, u32[]{:S(2)}) collective-permute-start(s32[3]{0:T(128)S(1)} %pad_add_fusion.4), channel_id=1, source_target_pairs={{0,8},{4,12},{8,16},{12,20},{16,24},{20,28},{24,32},{28,36},{32,40... | collective-permute-start | bytes 44 | tf_op jit(solution)/shard_map/ppermute | solution.py:18
  208.3 24.8 %collective-permute-start.13 = (bf16[2,128,1280]{2,1,0:T(8,128)(2,1)S(1)}, bf16[2,128,1280]{2,1,0:T(8,128)(2,1)S(1)}, u32[]{:S(2)}, u32[]{:S(2)}) collective-permute-start(bf16[2,128,1280]{2,1,0:T(8,128)(2,1)S(1)} %broadcast_select_fusion.4), channel_id=1, source_target_pairs={{0,2},{1,3},{2,0},{3,1},{4,6},{5,7},{6,4},{7,5},{8,10},{9,11},{10,... | collective-permute-start | bytes 1966088 | tf_op jit(solution)/shard_map/ppermute | solution.py:102
  233.2 31.0 %collective-permute-start.14 = (bf16[2,128,1280]{2,1,0:T(8,128)(2,1)S(1)}, bf16[2,128,1280]{2,1,0:T(8,128)(2,1)S(1)}, u32[]{:S(2)}, u32[]{:S(2)}) collective-permute-start(bf16[2,128,1280]{2,1,0:T(8,128)(2,1)S(1)} %broadcast_select_fusion.5), channel_id=1, source_target_pairs={{0,1},{1,0},{2,3},{3,2},{4,5},{5,4},{6,7},{7,6},{8,9},{9,8},{10,11... | collective-permute-start | bytes 1966088 | tf_op jit(solution)/shard_map/ppermute | solution.py:102
  269.1 47.9 %collective-permute-start.1 = (bf16[3,128,2560]{2,1,0:T(8,128)(2,1)}, bf16[3,128,2560]{2,1,0:T(8,128)(2,1)}, u32[]{:S(2)}, u32[]{:S(2)}) collective-permute-start(bf16[3,128,2560]{2,1,0:T(8,128)(2,1)} %gather_fusion.4), channel_id=1, source_target_pairs={{0,8},{4,12},{8,16},{12,20},{16,24},{20,28},{24,32},{28,36},{32,40... | collective-permute-start | bytes 5898248 | tf_op jit(solution)/shard_map/ppermute | solution.py:18
  276.7 58.5 %collective-permute-start.3 = (bf16[3,128,2560]{2,1,0:T(8,128)(2,1)}, bf16[3,128,2560]{2,1,0:T(8,128)(2,1)}, u32[]{:S(2)}, u32[]{:S(2)}) collective-permute-start(bf16[3,128,2560]{2,1,0:T(8,128)(2,1)} %gather_fusion.5), channel_id=1, source_target_pairs={{0,4},{4,8},{8,12},{12,16},{16,20},{20,24},{24,28},{28,32},{32,36}... | collective-permute-start | bytes 5898248 | tf_op jit(solution)/shard_map/ppermute | solution.py:18
  283.2 53.7 %collective-permute-start.5 = (bf16[3,128,2560]{2,1,0:T(8,128)(2,1)}, bf16[3,128,2560]{2,1,0:T(8,128)(2,1)}, u32[]{:S(2)}, u32[]{:S(2)}) collective-permute-start(bf16[3,128,2560]{2,1,0:T(8,128)(2,1)} %gather_fusion.6), channel_id=1, source_target_pairs={{4,0},{8,4},{12,8},{16,12},{20,16},{24,20},{28,24},{32,28},{36,32}... | collective-permute-start | bytes 5898248 | tf_op jit(solution)/shard_map/ppermute | solution.py:18
  287.3 12.8 %slice-start = ((s8[5242880]{0:T(1024)(128)(4,1)}), s8[1048576]{0:T(1024)(128)(4,1)S(1)}, s32[]{:S(2)}) async-start(s8[5242880]{0:T(1024)(128)(4,1)} %bitcast.185), calls=%async_computation.3 | async-start | bytes 2097152
  292.0 8.1 %slice-start.1 = ((s8[5242880]{0:T(1024)(128)(4,1)}), s8[4194304]{0:T(1024)(128)(4,1)S(1)}, s32[]{:S(2)}) async-start(s8[5242880]{0:T(1024)(128)(4,1)} %bitcast.185), calls=%async_computation.4 | async-start | bytes 8388608
  292.0 61.8 %collective-permute-start.7 = (bf16[3,128,2560]{2,1,0:T(8,128)(2,1)}, bf16[3,128,2560]{2,1,0:T(8,128)(2,1)S(1)}, u32[]{:S(2)}, u32[]{:S(2)}) collective-permute-start(bf16[3,128,2560]{2,1,0:T(8,128)(2,1)} %gather_fusion.7), channel_id=1, source_target_pairs={{8,0},{12,4},{16,8},{20,12},{24,16},{28,20},{32,24},{36,28},{40,32... | collective-permute-start | bytes 5898248 | tf_op jit(solution)/shard_map/ppermute | solution.py:18
  338.5 20.6 %slice-start.2 = ((bf16[256,3840]{1,0:T(8,128)(2,1)}), bf16[256,1280]{1,0:T(8,128)(2,1)S(1)}, s32[]{:S(2)}) async-start(bf16[256,3840]{1,0:T(8,128)(2,1)} %copy-done.4), calls=%async_computation.5 | async-start | bytes 1310720 | tf_op jit(solution)/shard_map/slice | solution.py:114
  338.5 20.6 %copy-start.11 = (bf16[2,128,1280]{2,1,0:T(8,128)(2,1)S(1)}, bf16[2,128,1280]{2,1,0:T(8,128)(2,1)}, u32[]{:S(2)}) copy-start(bf16[2,128,1280]{2,1,0:T(8,128)(2,1)} %custom-call.17) | copy-start | bytes 1966084
  338.6 20.6 %copy-start.12 = (s32[2]{0:T(128)S(1)}, s32[2]{0:T(128)}, u32[]{:S(2)}) copy-start(s32[2]{0:T(128)} %param.16) | copy-start | bytes 28
  354.1 5.0 %copy-start.2 = (bf16[22,128,2560]{2,1,0:T(8,128)(2,1)}, bf16[22,128,2560]{2,1,0:T(8,128)(2,1)S(1)}, u32[]{:S(2)}) copy-start(bf16[22,128,2560]{2,1,0:T(8,128)(2,1)S(1)} %constant_dynamic-update-slice_fusion.1) | copy-start | bytes 43253764
  486.0 3.9 copy-start.1
Sparse Core Ops, SparseCore 0:
  134.4 58.4 all-gather.2
  208.2 61.5 all-gather.4
